TPU v7x, 32 devices: a whole 2x2x4 slice. The times are simulated.
32 devices in a mesh: groups: 2 (over y), replica: 4 (over z), tensor: 4 (over x, core).
Axes of the slice: x: 2, y: 2, z: 4, core: 2. Of those that a mesh axis runs over, the one named last changes fastest.
Arguments:
- queries: bfloat16 [8, 128, 8192], P(('groups', 'replica'), None, 'tensor'), parts along dimension 0, may hold values from -12 to 12
- suffix_kv: bfloat16 [8, 2, 128, 1024], P(('groups', 'replica'), None, None, 'tensor'), parts along dimension 0, may hold values from -12 to 12
- page_pool: bfloat16 [96, 2, 128, 1024], P(('groups', 'replica'), None, 'tensor'), parts along dimension 0, may hold values from -6 to 6
- offsets: int32 [8, 8], P('groups'), parts along dimension 0, may hold values from 1 to 3, as said below
- slots: int32 [8, 8], P('groups'), parts along dimension 0, may hold values from 0 to 11, as said below
- prefix_len: int32 [8], P('groups'), parts along dimension 0, may hold values from 1 to 1024, 2048 in all
Outputs:
- attended: bfloat16 [8, 128, 8192], P(('groups', 'replica'), None, 'tensor'), parts along dimension 0
There are 2 independent parts, one for each index of `groups`. A program takes and returns all parts, laid end to end along the dimension named above; each array names one. Nothing has to cross between parts.
Inputs may be any that keep to these rules, and one draw needn't show every extreme that they name: Page p of request r is held by replica (r - offsets[r, p]) mod 4; one request takes at most 4 pages from one holder, and exactly 4 from some holder. `slots`: the prefix pages of one request are distinct pool entries. `prefix_len`: the longest prefix fills all 8 pages.
All inputs are finite; a program needn't handle non-finite values.
Results may differ from a plain program's by a relative error of at most 0.0034.
Values may be sent and summed in bfloat16 or wider, within the bound.
No kernel may reach another device: no remote copies, remote signals or barrier semaphores. Data moves between devices by JAX's collectives and lax.ppermute only.
A program may use at most 64 MiB of HBM per device.

v0:
```python
import math
import jax
import jax.numpy as jnp
from jax import lax
from jax.sharding import PartitionSpec as P

HEADS = 64
KV_HEADS = 8
HEAD_DIM = 128
NEG_FILL = -1e30


def passed_along(value, axis, steps):
    count = lax.axis_size(axis)
    pairs = [(source, (source + steps) % count) for source in range(count)]
    return lax.ppermute(value, axis, pairs)


def absorb(state_now, scores, visible, values):
    run_max, run_sum, run_acc = state_now
    masked = jnp.where(visible, scores, NEG_FILL)
    new_max = jnp.maximum(run_max, jnp.max(masked, axis=-1))
    weights = jnp.where(visible, jnp.exp(masked - new_max[..., None]), 0.0)
    rescale = jnp.exp(run_max - new_max)
    run_sum = run_sum * rescale + jnp.sum(weights, axis=-1)
    update = jnp.einsum(
        "kgqc,ckd->kgqd", weights.astype(jnp.bfloat16), values, preferred_element_type=jnp.float32
    )
    run_acc = run_acc * rescale[..., None] + update
    return (new_max, run_sum, run_acc)


def pack_pages(pool_part, offsets, slots, holder, replicas, span_count, slot_cap):
    distances = jnp.arange(1, span_count + 1, dtype=jnp.int32)
    readers = (holder + distances) % replicas
    off_rows = jnp.take(offsets, readers, axis=0)
    slot_rows = jnp.take(slots, readers, axis=0)
    matched = (off_rows == distances[:, None]).astype(jnp.int32)
    ranking = jnp.cumsum(matched, axis=1) - 1
    places = jnp.arange(slot_cap, dtype=jnp.int32)
    picked = matched[:, None, :] * (ranking[:, None, :] == places[None, :, None]).astype(jnp.int32)
    chosen = jnp.sum(picked * slot_rows[:, None, :], axis=2)
    gathered = jnp.take(pool_part, chosen.reshape(-1), axis=0)
    return gathered.reshape((span_count, slot_cap) + pool_part.shape[1:])


def page_index(own_offsets, slot_cap):
    page_count = own_offsets.shape[0]
    same_holder = own_offsets[:, None] == own_offsets[None, :]
    counter = jnp.arange(page_count, dtype=jnp.int32)
    earlier = counter[None, :] < counter[:, None]
    ranking = jnp.sum((same_holder & earlier).astype(jnp.int32), axis=1)
    return (own_offsets - 1) * slot_cap + ranking


def on_device(queries, suffix_kv, page_pool, offsets, slots, prefix_len):
    replicas = lax.axis_size("replica")
    reader = lax.axis_index("replica")
    span_count = min(8, replicas - 1)
    page_count = offsets.shape[1]
    slot_cap = (page_count + span_count - 1) // span_count + 1
    own_offsets = lax.dynamic_index_in_dim(offsets, reader, 0, keepdims=False)
    own_length = lax.dynamic_index_in_dim(prefix_len, reader, 0, keepdims=False)
    source = lax.all_to_all(page_pool, "tensor", split_axis=3, concat_axis=2, tiled=True)
    payload = pack_pages(source, offsets, slots, reader, replicas, span_count, slot_cap)
    arrivals = []
    for distance in range(1, span_count + 1):
        arrivals.append(passed_along(payload[distance - 1], "replica", distance))
    arrived = jnp.stack(arrivals)
    flattened = arrived.reshape((span_count * slot_cap,) + arrived.shape[2:])
    fetched = jnp.take(flattened, page_index(own_offsets, slot_cap), axis=0)
    width = fetched.shape[3]
    kv_local = width // HEAD_DIM
    group = HEADS // KV_HEADS
    suffix_rows = queries.shape[1]
    prefix_rows = page_count * fetched.shape[2]
    scale = HEAD_DIM ** (-0.5)
    query_heads = queries[0].reshape(suffix_rows, kv_local, group, HEAD_DIM)
    suffix_keys = suffix_kv[0, 0].reshape(suffix_rows, kv_local, HEAD_DIM)
    suffix_vals = suffix_kv[0, 1].reshape(suffix_rows, kv_local, HEAD_DIM)
    initial = (
        jnp.full((kv_local, group, suffix_rows), NEG_FILL, jnp.float32),
        jnp.zeros((kv_local, group, suffix_rows), jnp.float32),
        jnp.zeros((kv_local, group, suffix_rows, HEAD_DIM), jnp.float32),
    )
    suffix_scores = (
        jnp.einsum("qkgd,ckd->kgqc", query_heads, suffix_keys, preferred_element_type=jnp.float32)
        * scale
    )
    query_pos = jnp.arange(suffix_rows, dtype=jnp.int32)
    causal = query_pos[:, None] >= query_pos[None, :]
    state_now = absorb(initial, suffix_scores, causal, suffix_vals)
    block_rows = math.gcd(prefix_rows, 512)
    block_count = prefix_rows // block_rows
    prefix_keys = fetched[:, 0].reshape(block_count, block_rows, kv_local, HEAD_DIM)
    prefix_vals = fetched[:, 1].reshape(block_count, block_rows, kv_local, HEAD_DIM)
    block_pos = jnp.arange(block_rows, dtype=jnp.int32)

    def visit(state_in, pieces):
        keys_block, vals_block, first_row = pieces
        block_scores = (
            jnp.einsum(
                "qkgd,ckd->kgqc", query_heads, keys_block, preferred_element_type=jnp.float32
            )
            * scale
        )
        visible = first_row + block_pos < own_length
        return (absorb(state_in, block_scores, visible, vals_block), None)

    starts = jnp.arange(block_count, dtype=jnp.int32) * block_rows
    state_now, unused = lax.scan(visit, state_now, (prefix_keys, prefix_vals, starts))
    run_max, run_sum, run_acc = state_now
    result = run_acc / run_sum[..., None]
    result = result.transpose(2, 0, 1, 3).reshape(1, suffix_rows, kv_local * group * HEAD_DIM)
    return result.astype(jnp.bfloat16)


def solution(mesh):
    in_specs = (
        P(("groups", "replica"), None, "tensor"),
        P(("groups", "replica"), None, None, "tensor"),
        P(("groups", "replica"), None, "tensor", None),
        P("groups", None),
        P("groups", None),
        P("groups"),
    )
    out_specs = P(("groups", "replica"), None, "tensor")
    return jax.shard_map(
        on_device, mesh=mesh, in_specs=in_specs, out_specs=out_specs, check_vma=False
    )
```

profile of v0, /device:TPU:9, one launch (start us, length us, event | category | flops | bytes accessed | tf_op | source)
XLA Modules:
  0.0 132.8 jit_solution(631455684307266697)
XLA Ops:
  0.0 12.7 %copy.73 = bf16[12,2,32,1024]{2,0,1,3:T(8,128)(2,1)} copy(bf16[12,2,32,1024]{3,2,1,0:T(8,128)(2,1)} %param.12) | data formatting | bytes 3145728 | tf_op args[2]
  12.7 8.9 %reshape.178 = bf16[4,2,98304]{2,1,0:T(2,128)(2,1)} reshape(bf16[1024,2,12,32]{3,2,1,0:T(8,128)(2,1)} %bitcast.95) | data formatting | bytes 3145728
  21.6 4.3 %all-to-all-start = ((bf16[4,2,98304]{2,1,0:T(2,128)(2,1)}), bf16[4,2,98304]{2,1,0:T(2,128)(2,1)S(1)}, u32[]{:S(2)}, u32[]{:S(2)}) async-start(bf16[4,2,98304]{2,1,0:T(2,128)(2,1)} %reshape.178), calls=%async_computation | async-start | bytes 3145728 | tf_op jit(solution)/shard_map/all_to_all | solution.py:64
  26.0 0.6 gather_fusion.2
  26.5 0.6 gather_fusion.3
  27.2 0.2 reduce_window_sum.11
  27.4 0.1 multiply_reduce_fusion
  27.8 0.2 convert_reduce_fusion
  28.0 0.3 copy.67
  28.4 0.4 fusion.38
  28.8 0.2 fusion.21
  29.1 16.0 %all-to-all-done = bf16[4,2,98304]{2,1,0:T(2,128)(2,1)S(1)} async-done(((bf16[4,2,98304]{2,1,0:T(2,128)(2,1)}), bf16[4,2,98304]{2,1,0:T(2,128)(2,1)S(1)}, u32[]{:S(2)}, u32[]{:S(2)}) %all-to-all-start) | async-done | bytes 1572896 | tf_op jit(solution)/shard_map/all_to_all | solution.py:64
  45.1 7.1 %reshape.179 = bf16[1024,2,12,32]{3,2,1,0:T(8,128)(2,1)} reshape(bf16[4,2,98304]{2,1,0:T(2,128)(2,1)S(1)} %all-to-all-done) | data formatting | bytes 3145728
  52.2 9.6 %copy.91 = bf16[12,2,32,4,256]{4,3,2,1,0:T(4,128)(2,1)S(1)} copy(bf16[12,2,32,4,256]{2,0,1,4,3:T(8,128)(2,1)} %bitcast.94) | data formatting | bytes 3145728 | tf_op jit(solution)/shard_map/all_to_all | solution.py:64
  61.7 1.5 %copy.75 = bf16[12,2,4,32,256]{4,3,2,1,0:T(8,128)(2,1)} copy(bf16[12,2,4,32,256]{4,2,3,1,0:T(4,128)(2,1)S(1)} %bitcast.96) | data formatting | bytes 3145728 | tf_op jit(solution)/shard_map/all_to_all | solution.py:64
  63.2 2.1 %gather_fusion = bf16[12,2,128,256]{3,2,1,0:T(8,128)(2,1)S(1)} fusion(bf16[12,2,128,256]{3,2,1,0:T(8,128)(2,1)} %bitcast.97, s32[1024]{0:T(1024)S(1)} %pad_clamp_fusion.1), kind=kCustom, calls=%fused_computation.2 | custom fusion | bytes 3145776 | tf_op jit(solution)/shard_map/jit(_take)/gather | solution.py:43
  65.3 0.2 broadcast_select_fusion
  65.5 1.1 fusion.35
  66.6 1.3 collective-permute-start
  67.9 1.0 collective-permute-start.1
  68.9 1.5 %collective-permute-start.2 = (bf16[4,2,128,256]{3,2,1,0:T(8,128)(2,1)S(1)}, bf16[4,2,128,256]{3,2,1,0:T(8,128)(2,1)}, u32[]{:S(2)}, u32[]{:S(2)}) collective-permute-start(bf16[4,2,128,256]{3,2,1,0:T(8,128)(2,1)S(1)} %get-tuple-element.151), channel_id=1, source_target_pairs={{0,12},{4,0},{8,4},{12,8},{1,13},{5,1},{9,5},{13,9},{2,14},{6,2},{... | collective-permute-start | bytes 1572872 | tf_op jit(solution)/shard_map/ppermute | solution.py:16
  70.4 0.3 copy.77
  70.8 0.6 dynamic_slice.19
  71.4 1.5 %convolution_add_fusion = f32[2,8,128,128]{3,2,1,0:T(8,128)} fusion(bf16[128,2,128,1]{0,2,3,1:T(8,128)(2,1)S(1)} %bitcast.102, f32[2,8,128,128]{2,3,1,0:T(8,128)S(1)} %get-tuple-element.160, f32[2,8,128]{2,1,0:T(8,128)S(1)} %get-tuple-element.157, f32[2,8,128]{2,1,0:T(8,128)S(1)} %broadcast_maximum_fusion, pred[128,128]{0,1:T(8,128)(4,1)S(1)} %iota_compare_fusion), kind=kOutput, calls=%fused_computation.30 | convolution fusion | flops 68157440 | bytes 2195456 | tf_op jit(solution)/shard_map/kgqc,ckd->kgqd/dot_general | solution.py:26
  72.9 6.5 %collective-permute-done = bf16[4,2,128,256]{3,2,1,0:T(8,128)(2,1)S(1)} collective-permute-done((bf16[4,2,128,256]{3,2,1,0:T(8,128)(2,1)}, bf16[4,2,128,256]{3,2,1,0:T(8,128)(2,1)S(1)}, u32[]{:S(2)}, u32[]{:S(2)}) %collective-permute-start) | collective-permute-done | bytes 524320 | tf_op jit(solution)/shard_map/ppermute | solution.py:16
  79.4 32.9 %collective-permute-done.1 = bf16[4,2,128,256]{3,2,1,0:T(8,128)(2,1)} collective-permute-done((bf16[4,2,128,256]{3,2,1,0:T(8,128)(2,1)}, bf16[4,2,128,256]{3,2,1,0:T(8,128)(2,1)}, u32[]{:S(2)}, u32[]{:S(2)}) %collective-permute-start.1) | collective-permute-done | bytes 524320 | tf_op jit(solution)/shard_map/ppermute | solution.py:16
  112.3 3.1 %collective-permute-done.2 = bf16[4,2,128,256]{3,2,1,0:T(8,128)(2,1)} collective-permute-done((bf16[4,2,128,256]{3,2,1,0:T(8,128)(2,1)S(1)}, bf16[4,2,128,256]{3,2,1,0:T(8,128)(2,1)}, u32[]{:S(2)}, u32[]{:S(2)}) %collective-permute-start.2) | collective-permute-done | bytes 524320 | tf_op jit(solution)/shard_map/ppermute | solution.py:16
  115.4 1.5 %pad_maximum_fusion = bf16[3,4,2,128,256]{4,3,2,1,0:T(8,128)(2,1)S(1)} fusion(bf16[1,4,2,128,256]{4,3,2,1,0:T(8,128)(2,1)} %bitcast.14, bf16[1,4,2,128,256]{4,3,2,1,0:T(8,128)(2,1)} %bitcast.13, bf16[1,4,2,128,256]{4,3,2,1,0:T(8,128)(2,1)} %bitcast.101), kind=kLoop, calls=%fused_computation.28 | loop fusion | flops 1572864 | bytes 3145728 | tf_op jit(solution)/shard_map/stack | solution.py:69
  116.9 0.6 gather_fusion.1
  117.5 0.2 broadcast_select_fusion.1
  117.8 0.1 reshape_squeeze.18
  118.1 0.8 copy-done.1
  118.9 12.1 %while.15 = (s32[]{:T(128)}, f32[2,8,128]{2,1,0:T(8,128)S(1)}, f32[2,8,128]{2,1,0:T(8,128)S(1)}, f32[2,8,128,128]{3,2,1,0:T(8,128)S(1)}, s32[2]{0:T(128)S(1)}, /...) while((s32[]{:T(128)}, f32[2,8,128]{2,1,0:T(8,128)S(1)}, ...), condition=%wide.region_8.10_spmd.clone, body=%wide.region_5.9_spmd.clone.sunk | while | flops 551031808 | bytes 16910460 | solution.py:111
  118.9 0.6 dynamic_slice.36
  119.5 1.2 fusion.50
  120.7 0.4 constant_dynamic-slice_fusion.4
  121.1 0.8 bitcast_reduce_fusion.2
  121.9 1.1 fusion.51
  123.1 1.9 %fusion.52 = f32[2,8,128,128]{3,2,1,0:T(8,128)S(1)} fusion(f32[2,512,128,8]{2,1,3,0:T(8,128)S(1)} %get-tuple-element.226, f32[2,8,128]{2,1,0:T(8,128)S(1)} %max.5, pred[512]{0:T(512)(128)(4,1)S(1)} %fusion.50, f32[2,8,128,128]{3,2,1,0:T(8,128)S(1)} %get-tuple-element.243, f32[2,8,128]{2,1,0:T(8,128)S(1)} %get-tuple-element.228, ...), kind=kOutput, calls=%fused_computation.15.clone.1 | convolution fusion | flops 274202624 | bytes 6570496 | tf_op jit(solution)/shard_map/while/body/eval_jaxpr/kgqc,ckd->kgqd/dot_general | solution.py:26
  125.0 0.6 dynamic_slice.36
  125.6 1.2 fusion.50
  126.8 0.4 constant_dynamic-slice_fusion.4
  127.2 0.8 bitcast_reduce_fusion.2
  127.9 1.1 fusion.51
  129.1 1.9 %fusion.52 = f32[2,8,128,128]{3,2,1,0:T(8,128)S(1)} fusion(f32[2,512,128,8]{2,1,3,0:T(8,128)S(1)} %get-tuple-element.226, f32[2,8,128]{2,1,0:T(8,128)S(1)} %max.5, pred[512]{0:T(512)(128)(4,1)S(1)} %fusion.50, f32[2,8,128,128]{3,2,1,0:T(8,128)S(1)} %get-tuple-element.243, f32[2,8,128]{2,1,0:T(8,128)S(1)} %get-tuple-element.228, ...), kind=kOutput, calls=%fused_computation.15.clone.1 | convolution fusion | flops 274202624 | bytes 6570496 | tf_op jit(solution)/shard_map/while/body/eval_jaxpr/kgqc,ckd->kgqd/dot_general | solution.py:26
  131.0 0.3 fusion.25
  131.4 0.3 copy.79
  131.7 1.0 convert_element_type.35
  (43 shorter events, 1.0 us)
Async XLA Ops:
  0.0 26.5 %copy-start = (s32[4,8]{1,0:T(4,128)S(1)}, s32[4,8]{1,0:T(4,128)}, u32[]{:S(2)}) copy-start(s32[4,8]{1,0:T(4,128)} %param.14) | copy-start | bytes 388
  12.7 13.3 %copy-start.4 = (s32[4,8]{1,0:T(4,128)S(1)}, s32[4,8]{1,0:T(4,128)}, u32[]{:S(2)}) copy-start(s32[4,8]{1,0:T(4,128)} %param.13) | copy-start | bytes 388
  12.7 15.3 %copy-start.2 = (bf16[1,128,2048]{2,1,0:T(8,128)(2,1)S(1)}, bf16[1,128,2048]{2,1,0:T(8,128)(2,1)}, u32[]{:S(2)}) copy-start(bf16[1,128,2048]{2,1,0:T(8,128)(2,1)} %param.10) | copy-start | bytes 1572868
  21.6 6.7 %copy-start.5 = (bf16[1,2,128,256]{3,2,1,0:T(8,128)(2,1)S(1)}, bf16[1,2,128,256]{3,2,1,0:T(8,128)(2,1)}, u32[]{:S(2)}) copy-start(bf16[1,2,128,256]{3,2,1,0:T(8,128)(2,1)} %param.11) | copy-start | bytes 393220
  21.6 23.6 %all-to-all-start = ((bf16[4,2,98304]{2,1,0:T(2,128)(2,1)}), bf16[4,2,98304]{2,1,0:T(2,128)(2,1)S(1)}, u32[]{:S(2)}, u32[]{:S(2)}) async-start(bf16[4,2,98304]{2,1,0:T(2,128)(2,1)} %reshape.178), calls=%async_computation | async-start | bytes 3145728 | tf_op jit(solution)/shard_map/all_to_all | solution.py:64
  65.3 5.5 %copy-start.6 = (s32[4]{0:T(128)S(1)}, s32[4]{0:T(128)}, u32[]{:S(2)}) copy-start(s32[4]{0:T(128)} %param.15) | copy-start | bytes 52
  66.6 12.8 %collective-permute-start = (bf16[4,2,128,256]{3,2,1,0:T(8,128)(2,1)}, bf16[4,2,128,256]{3,2,1,0:T(8,128)(2,1)S(1)}, u32[]{:S(2)}, u32[]{:S(2)}) collective-permute-start(bf16[4,2,128,256]{3,2,1,0:T(8,128)(2,1)} %get-tuple-element.150), channel_id=1, source_target_pairs={{0,4},{4,8},{8,12},{12,0},{1,5},{5,9},{9,13},{13,1},{2,6},{6,10},{... | collective-permute-start | bytes 1572872 | tf_op jit(solution)/shard_map/ppermute | solution.py:16
  67.9 44.4 %collective-permute-start.1 = (bf16[4,2,128,256]{3,2,1,0:T(8,128)(2,1)}, bf16[4,2,128,256]{3,2,1,0:T(8,128)(2,1)}, u32[]{:S(2)}, u32[]{:S(2)}) collective-permute-start(bf16[4,2,128,256]{3,2,1,0:T(8,128)(2,1)} %get-tuple-element.152), channel_id=1, source_target_pairs={{0,8},{4,12},{8,0},{12,4},{1,9},{5,13},{9,1},{13,5},{2,10},{6,14},... | collective-permute-start | bytes 1572872 | tf_op jit(solution)/shard_map/ppermute | solution.py:16
  68.9 46.4 %collective-permute-start.2 = (bf16[4,2,128,256]{3,2,1,0:T(8,128)(2,1)S(1)}, bf16[4,2,128,256]{3,2,1,0:T(8,128)(2,1)}, u32[]{:S(2)}, u32[]{:S(2)}) collective-permute-start(bf16[4,2,128,256]{3,2,1,0:T(8,128)(2,1)S(1)} %get-tuple-element.151), channel_id=1, source_target_pairs={{0,12},{4,0},{8,4},{12,8},{1,13},{5,1},{9,5},{13,9},{2,14},{6,2},{... | collective-permute-start | bytes 1572872 | tf_op jit(solution)/shard_map/ppermute | solution.py:16
  79.4 36.0 %copy-start.3 = (bf16[4,2,128,256]{3,2,1,0:T(8,128)(2,1)}, bf16[4,2,128,256]{3,2,1,0:T(8,128)(2,1)S(1)}, u32[]{:S(2)}) copy-start(bf16[4,2,128,256]{3,2,1,0:T(8,128)(2,1)S(1)} %collective-permute-done) | copy-start | bytes 1572868
  117.7 1.2 copy-start.1
where the time goes:
time: 133 us
  waiting for transfers between devices  58.5 us (44%)
  local copies, waits for them, and re-layouts  50.6 us (38%)
  starting transfers between devices  8.11 us (6%)
  other arithmetic  7.99 us (6%)
  matrix products  7.18 us (5%)
    ppermute x3, waiting for transfers between devices, passed_along(): return lax.ppermute(value, axis, pairs)  42.4 us
    unnamed x21, local copies, waits for them, and re-layouts  30.3 us
    all_to_all x1, waiting for transfers between devices, on_device(): lax.all_to_all(page_pool, 'tensor', split_axis=3, concat_axis=2, tiled=True)  16 us
    all_to_all x2, local copies, waits for them, and re-layouts, on_device(): lax.all_to_all(page_pool, 'tensor', split_axis=3, concat_axis=2, tiled=True)  11 us
    dot_general x3, matrix products, absorb(): jnp.einsum('kgqc,ckd->kgqd', weights.astype(jnp.bfloat16), values, prefer...  5.31 us
    all_to_all x1, starting transfers between devices, on_device(): lax.all_to_all(page_pool, 'tensor', split_axis=3, concat_axis=2, tiled=True)  4.34 us
    ppermute x3, starting transfers between devices, passed_along(): return lax.ppermute(value, axis, pairs)  3.78 us
  transfers between devices with their start and end apart: 4, of which 4 were waited for; matrix products, arithmetic and copies ran while one was open for 4% of the time, Pallas kernels for 0%

commit v1 on v0

--- a/solution.py
+++ b/solution.py
@@ -8,6 +8,12 @@
 KV_HEADS = 8
 HEAD_DIM = 128
 NEG_FILL = -1e30
+
+
+def stacked_exchange(shard, mesh_axis, split, join):
+    pieces = jnp.split(shard, lax.axis_size(mesh_axis), axis=split)
+    incoming = lax.all_to_all(jnp.stack(pieces), mesh_axis, 0, 0)
+    return jnp.concatenate(incoming, axis=join)
 
 
 def passed_along(value, axis, steps):
@@ -61,7 +67,7 @@
     slot_cap = (page_count + span_count - 1) // span_count + 1
     own_offsets = lax.dynamic_index_in_dim(offsets, reader, 0, keepdims=False)
     own_length = lax.dynamic_index_in_dim(prefix_len, reader, 0, keepdims=False)
-    source = lax.all_to_all(page_pool, "tensor", split_axis=3, concat_axis=2, tiled=True)
+    source = stacked_exchange(page_pool, "tensor", 3, 2)
     payload = pack_pages(source, offsets, slots, reader, replicas, span_count, slot_cap)
     arrivals = []
     for distance in range(1, span_count + 1):

time: 133 us -> 100 us (0.75)
  the two profiles are of different devices: /device:TPU:9 before, /device:TPU:0 now
where the time goes in v1:
time: 100 us; the launch traced here: 99.9 us
  waiting for transfers between devices  59 us (59%)
  local copies, waits for them, and re-layouts  13.9 us (14%)
  starting transfers between devices  9.73 us (10%)
  other arithmetic  9.64 us (10%)
  matrix products  7.19 us (7%)
    ppermute x3, waiting for transfers between devices, passed_along(): return lax.ppermute(value, axis, pairs)  42.1 us
    all_to_all x1, waiting for transfers between devices, stacked_exchange(): incoming = lax.all_to_all(jnp.stack(pieces), mesh_axis, 0, 0)  16.9 us
    ppermute x3, starting transfers between devices, passed_along(): return lax.ppermute(value, axis, pairs)  5.39 us
    dot_general x3, matrix products, absorb(): jnp.einsum('kgqc,ckd->kgqd', weights.astype(jnp.bfloat16), values, prefer...  5.32 us
    all_to_all x1, starting transfers between devices, stacked_exchange(): incoming = lax.all_to_all(jnp.stack(pieces), mesh_axis, 0, 0)  4.34 us
    lt x2, other arithmetic, visit(): visible = first_row + block_pos < own_length  2.68 us
    reduce_sum x3, other arithmetic, absorb(): run_sum = run_sum * rescale + jnp.sum(weights, axis=-1)  2.51 us
    gather x1, local copies, waits for them, and re-layouts, pack_pages(): gathered = jnp.take(pool_part, chosen.reshape(-1), axis=0)  2.05 us
  transfers between devices with their start and end apart: 4, of which 4 were waited for; matrix products, arithmetic and copies ran while one was open for 6% of the time, Pallas kernels for 0%

profile of v1, /device:TPU:0, one launch (start us, length us, event | category | flops | bytes accessed | tf_op | source)
XLA Modules:
  0.0 99.9 jit_solution(11257995626010672255)
XLA Ops:
  0.0 1.6 %slice_bitcast_fusion.3 = (bf16[1,12,2,32,256]{4,3,2,1,0:T(8,128)(2,1)S(1)}, bf16[1,12,2,32,256]{4,3,2,1,0:T(8,128)(2,1)S(1)}, bf16[1,12,2,32,256]{4,3,2,1,0:T(8,128)(2,1)S(1)}, bf16[1,12,2,32,256]{4,3,2,1,0:T(8,128)(2,1)S(1)}) fusion(bf16[12,2,32,1024]{3,2,1,0:T(8,128)(2,1)} %param.12), kind=kLoop, calls=%fused_computation.47 | loop fusion | bytes 3145728 | tf_op jit(solution)/shard_map/stack | solution.py:15
  1.6 1.4 %pad_maximum_fusion = bf16[4,12,2,32,256]{4,3,2,1,0:T(8,128)(2,1)} fusion(bf16[1,12,2,32,256]{4,3,2,1,0:T(8,128)(2,1)S(1)} %get-tuple-element.146, bf16[1,12,2,32,256]{4,3,2,1,0:T(8,128)(2,1)S(1)} %get-tuple-element.147, bf16[1,12,2,32,256]{4,3,2,1,0:T(8,128)(2,1)S(1)} %get-tuple-element.145, bf16[1,12,2,32,256]{4,3,2,1,0:T(8,128)(2,1)S(1)} %get-tuple-element.144), kind=kLoop, calls=%fused_computation.28 | loop fusion | flops 2359296 | bytes 3145728 | tf_op jit(solution)/shard_map/stack | solution.py:15
  2.9 4.3 %all-to-all-start = ((bf16[4,12,2,32,256]{4,3,2,1,0:T(8,128)(2,1)}), bf16[4,12,2,32,256]{4,3,2,1,0:T(8,128)(2,1)S(1)}, u32[]{:S(2)}, u32[]{:S(2)}) async-start(bf16[4,12,2,32,256]{4,3,2,1,0:T(8,128)(2,1)} %pad_maximum_fusion), calls=%async_computation | async-start | bytes 3145728 | tf_op jit(solution)/shard_map/all_to_all | solution.py:15
  7.3 0.6 gather_fusion.3
  7.9 0.6 gather_fusion.2
  8.5 0.2 reduce_window_sum.11
  8.8 0.1 multiply_reduce_fusion
  9.2 0.2 convert_reduce_fusion
  9.4 0.1 copy.73
  9.5 0.3 copy.49
  9.8 0.4 fusion.38
  10.2 0.2 fusion.21
  10.5 16.9 %all-to-all-done = bf16[4,12,2,32,256]{4,3,2,1,0:T(8,128)(2,1)S(1)} async-done(((bf16[4,12,2,32,256]{4,3,2,1,0:T(8,128)(2,1)}), bf16[4,12,2,32,256]{4,3,2,1,0:T(8,128)(2,1)S(1)}, u32[]{:S(2)}, u32[]{:S(2)}) %all-to-all-start) | async-done | bytes 1572896 | tf_op jit(solution)/shard_map/all_to_all | solution.py:15
  27.4 1.3 %copy.55 = bf16[4,12,2,32,256]{4,3,0,2,1:T(8,128)(2,1)} copy(bf16[4,12,2,32,256]{4,3,2,1,0:T(8,128)(2,1)S(1)} %all-to-all-done) | data formatting | bytes 3145728 | tf_op jit(solution)/shard_map/all_to_all | solution.py:15
  28.7 2.1 %gather_fusion = bf16[12,2,128,256]{3,2,1,0:T(8,128)(2,1)S(1)} fusion(bf16[12,2,128,256]{3,2,1,0:T(8,128)(2,1)} %bitcast.100, s32[1024]{0:T(1024)S(1)} %pad_clamp_fusion.1), kind=kCustom, calls=%fused_computation.2 | custom fusion | bytes 3145776 | tf_op jit(solution)/shard_map/jit(_take)/gather | solution.py:49
  30.8 0.2 broadcast_select_fusion
  31.0 1.1 %fusion.35 = (bf16[4,2,128,256]{3,2,1,0:T(8,128)(2,1)}, bf16[4,2,128,256]{3,2,1,0:T(8,128)(2,1)}, bf16[4,2,128,256]{3,2,1,0:T(8,128)(2,1)S(1)}) fusion(bf16[12,2,128,256]{3,2,1,0:T(8,128)(2,1)S(1)} %broadcast_select_fusion), kind=kLoop, calls=%fused_computation.84 | loop fusion | bytes 3145728 | tf_op jit(solution)/shard_map/slice | solution.py:74
  32.1 2.3 %collective-permute-start = (bf16[4,2,128,256]{3,2,1,0:T(8,128)(2,1)}, bf16[4,2,128,256]{3,2,1,0:T(8,128)(2,1)S(1)}, u32[]{:S(2)}, u32[]{:S(2)}) collective-permute-start(bf16[4,2,128,256]{3,2,1,0:T(8,128)(2,1)} %get-tuple-element.141), channel_id=1, source_target_pairs={{0,4},{4,8},{8,12},{12,0},{1,5},{5,9},{9,13},{13,1},{2,6},{6,10},{... | collective-permute-start | bytes 1572872 | tf_op jit(solution)/shard_map/ppermute | solution.py:22
  34.4 2.0 %collective-permute-start.2 = (bf16[4,2,128,256]{3,2,1,0:T(8,128)(2,1)}, bf16[4,2,128,256]{3,2,1,0:T(8,128)(2,1)}, u32[]{:S(2)}, u32[]{:S(2)}) collective-permute-start(bf16[4,2,128,256]{3,2,1,0:T(8,128)(2,1)} %get-tuple-element.142), channel_id=1, source_target_pairs={{0,12},{4,0},{8,4},{12,8},{1,13},{5,1},{9,5},{13,9},{2,14},{6,2},{... | collective-permute-start | bytes 1572872 | tf_op jit(solution)/shard_map/ppermute | solution.py:22
  36.5 1.0 %collective-permute-start.1 = (bf16[4,2,128,256]{3,2,1,0:T(8,128)(2,1)S(1)}, bf16[4,2,128,256]{3,2,1,0:T(8,128)(2,1)}, u32[]{:S(2)}, u32[]{:S(2)}) collective-permute-start(bf16[4,2,128,256]{3,2,1,0:T(8,128)(2,1)S(1)} %get-tuple-element.143), channel_id=1, source_target_pairs={{0,8},{4,12},{8,0},{12,4},{1,9},{5,13},{9,1},{13,5},{2,10},{6,14},... | collective-permute-start | bytes 1572872 | tf_op jit(solution)/shard_map/ppermute | solution.py:22
  37.5 0.3 copy.57
  37.8 0.7 dynamic_slice.19
  38.6 1.5 %convolution_add_fusion = f32[2,8,128,128]{3,2,1,0:T(8,128)} fusion(bf16[128,2,128,1]{0,2,3,1:T(8,128)(2,1)S(1)} %bitcast.105, f32[2,8,128,128]{2,3,1,0:T(8,128)S(1)} %get-tuple-element.155, f32[2,8,128]{2,1,0:T(8,128)S(1)} %get-tuple-element.152, f32[2,8,128]{2,1,0:T(8,128)S(1)} %broadcast_maximum_fusion, pred[128,128]{0,1:T(8,128)(4,1)S(1)} %iota_compare_fusion), kind=kOutput, calls=%fused_computation.31 | convolution fusion | flops 68157440 | bytes 2195456 | tf_op jit(solution)/shard_map/kgqc,ckd->kgqd/dot_general | solution.py:32
  40.1 9.4 %collective-permute-done = bf16[4,2,128,256]{3,2,1,0:T(8,128)(2,1)S(1)} collective-permute-done((bf16[4,2,128,256]{3,2,1,0:T(8,128)(2,1)}, bf16[4,2,128,256]{3,2,1,0:T(8,128)(2,1)S(1)}, u32[]{:S(2)}, u32[]{:S(2)}) %collective-permute-start) | collective-permute-done | bytes 524320 | tf_op jit(solution)/shard_map/ppermute | solution.py:22
  49.5 9.7 %collective-permute-done.2 = bf16[4,2,128,256]{3,2,1,0:T(8,128)(2,1)} collective-permute-done((bf16[4,2,128,256]{3,2,1,0:T(8,128)(2,1)}, bf16[4,2,128,256]{3,2,1,0:T(8,128)(2,1)}, u32[]{:S(2)}, u32[]{:S(2)}) %collective-permute-start.2) | collective-permute-done | bytes 524320 | tf_op jit(solution)/shard_map/ppermute | solution.py:22
  59.2 23.0 %collective-permute-done.1 = bf16[4,2,128,256]{3,2,1,0:T(8,128)(2,1)} collective-permute-done((bf16[4,2,128,256]{3,2,1,0:T(8,128)(2,1)S(1)}, bf16[4,2,128,256]{3,2,1,0:T(8,128)(2,1)}, u32[]{:S(2)}, u32[]{:S(2)}) %collective-permute-start.1) | collective-permute-done | bytes 524320 | tf_op jit(solution)/shard_map/ppermute | solution.py:22
  82.2 1.5 %pad_maximum_fusion.1 = bf16[3,4,2,128,256]{4,3,2,1,0:T(8,128)(2,1)S(1)} fusion(bf16[1,4,2,128,256]{4,3,2,1,0:T(8,128)(2,1)} %bitcast.17, bf16[1,4,2,128,256]{4,3,2,1,0:T(8,128)(2,1)} %bitcast.16, bf16[1,4,2,128,256]{4,3,2,1,0:T(8,128)(2,1)} %bitcast.104), kind=kLoop, calls=%fused_computation.29 | loop fusion | flops 1572864 | bytes 3145728 | tf_op jit(solution)/shard_map/stack | solution.py:75
  83.7 0.6 gather_fusion.1
  84.4 0.2 broadcast_select_fusion.1
  84.6 0.1 reshape_squeeze.19
  84.8 0.1 reshape_squeeze.18
  84.9 0.9 copy-done.1
  85.8 12.4 %while.15 = (s32[]{:T(128)}, f32[2,8,128]{2,1,0:T(8,128)S(1)}, f32[2,8,128]{2,1,0:T(8,128)S(1)}, f32[2,8,128,128]{3,2,1,0:T(8,128)S(1)}, s32[2]{0:T(128)S(1)}, /...) while((s32[]{:T(128)}, f32[2,8,128]{2,1,0:T(8,128)S(1)}, ...), condition=%wide.region_8.10_spmd.clone, body=%wide.region_5.9_spmd.clone.sunk | while | flops 551031808 | bytes 16910468 | solution.py:117
  85.8 0.6 dynamic_slice.36
  86.3 1.3 %fusion.50 = pred[512]{0:T(512)(128)(4,1)S(1)} fusion(s32[]{:T(128)} %get-tuple-element.250, s32[]{:T(128)} %bitcast.99), kind=kLoop, calls=%fused_computation.22.clone.1 | loop fusion | flops 1024 | bytes 520 | tf_op jit(solution)/shard_map/while/body/eval_jaxpr/lt | solution.py:113
  87.7 0.4 constant_dynamic-slice_fusion.4
  88.1 0.8 bitcast_reduce_fusion.2
  88.8 1.2 %fusion.51 = f32[2,8,128]{2,1,0:T(8,128)S(1)} fusion(f32[2,512,128,8]{2,1,3,0:T(8,128)S(1)} %get-tuple-element.221, f32[2,8,128]{2,1,0:T(8,128)S(1)} %max.5, pred[512]{0:T(512)(128)(4,1)S(1)} %fusion.50), kind=kLoop, calls=%fused_computation.11.clone.1 | loop fusion | flops 5240832 | bytes 4211200 | tf_op jit(solution)/shard_map/while/body/eval_jaxpr/reduce_sum | solution.py:31
  90.0 1.9 %fusion.52 = f32[2,8,128,128]{3,2,1,0:T(8,128)S(1)} fusion(f32[2,512,128,8]{2,1,3,0:T(8,128)S(1)} %get-tuple-element.221, f32[2,8,128]{2,1,0:T(8,128)S(1)} %max.5, pred[512]{0:T(512)(128)(4,1)S(1)} %fusion.50, f32[2,8,128,128]{3,2,1,0:T(8,128)S(1)} %get-tuple-element.238, f32[2,8,128]{2,1,0:T(8,128)S(1)} %get-tuple-element.223, ...), kind=kOutput, calls=%fused_computation.15.clone.1 | convolution fusion | flops 274202624 | bytes 6570496 | tf_op jit(solution)/shard_map/while/body/eval_jaxpr/kgqc,ckd->kgqd/dot_general | solution.py:32
  92.0 0.6 dynamic_slice.36
  92.5 1.3 %fusion.50 = pred[512]{0:T(512)(128)(4,1)S(1)} fusion(s32[]{:T(128)} %get-tuple-element.250, s32[]{:T(128)} %bitcast.99), kind=kLoop, calls=%fused_computation.22.clone.1 | loop fusion | flops 1024 | bytes 520 | tf_op jit(solution)/shard_map/while/body/eval_jaxpr/lt | solution.py:113
  93.9 0.4 constant_dynamic-slice_fusion.4
  94.3 0.8 bitcast_reduce_fusion.2
  95.0 1.2 %fusion.51 = f32[2,8,128]{2,1,0:T(8,128)S(1)} fusion(f32[2,512,128,8]{2,1,3,0:T(8,128)S(1)} %get-tuple-element.221, f32[2,8,128]{2,1,0:T(8,128)S(1)} %max.5, pred[512]{0:T(512)(128)(4,1)S(1)} %fusion.50), kind=kLoop, calls=%fused_computation.11.clone.1 | loop fusion | flops 5240832 | bytes 4211200 | tf_op jit(solution)/shard_map/while/body/eval_jaxpr/reduce_sum | solution.py:31
  96.2 1.9 %fusion.52 = f32[2,8,128,128]{3,2,1,0:T(8,128)S(1)} fusion(f32[2,512,128,8]{2,1,3,0:T(8,128)S(1)} %get-tuple-element.221, f32[2,8,128]{2,1,0:T(8,128)S(1)} %max.5, pred[512]{0:T(512)(128)(4,1)S(1)} %fusion.50, f32[2,8,128,128]{3,2,1,0:T(8,128)S(1)} %get-tuple-element.238, f32[2,8,128]{2,1,0:T(8,128)S(1)} %get-tuple-element.223, ...), kind=kOutput, calls=%fused_computation.15.clone.1 | convolution fusion | flops 274202624 | bytes 6570496 | tf_op jit(solution)/shard_map/while/body/eval_jaxpr/kgqc,ckd->kgqd/dot_general | solution.py:32
  98.2 0.3 fusion.25
  98.5 0.3 copy.59
  98.9 1.0 %convert_element_type.35 = bf16[1,128,2048]{2,1,0:T(8,128)(2,1)} reshape(bf16[128,2,8,128]{3,2,1,0:T(8,128)(2,1)S(1)} %copy.59) | data formatting | bytes 1048576 | tf_op jit(solution)/shard_map/convert_element_type | solution.py:121
  (41 shorter events, 0.7 us)
Async XLA Ops:
  0.0 7.3 %copy-start = (s32[4,8]{1,0:T(4,128)S(1)}, s32[4,8]{1,0:T(4,128)}, u32[]{:S(2)}) copy-start(s32[4,8]{1,0:T(4,128)} %param.14) | copy-start | bytes 388
  2.9 5.0 %copy-start.4 = (s32[4,8]{1,0:T(4,128)S(1)}, s32[4,8]{1,0:T(4,128)}, u32[]{:S(2)}) copy-start(s32[4,8]{1,0:T(4,128)} %param.13) | copy-start | bytes 388
  2.9 6.5 %copy-start.5 = (bf16[1,2,128,256]{3,2,1,0:T(8,128)(2,1)S(1)}, bf16[1,2,128,256]{3,2,1,0:T(8,128)(2,1)}, u32[]{:S(2)}) copy-start(bf16[1,2,128,256]{3,2,1,0:T(8,128)(2,1)} %param.11) | copy-start | bytes 393220
  2.9 6.6 %copy-start.2 = (bf16[1,128,2048]{2,1,0:T(8,128)(2,1)S(1)}, bf16[1,128,2048]{2,1,0:T(8,128)(2,1)}, u32[]{:S(2)}) copy-start(bf16[1,128,2048]{2,1,0:T(8,128)(2,1)} %param.10) | copy-start | bytes 1572868
  2.9 24.4 %all-to-all-start = ((bf16[4,12,2,32,256]{4,3,2,1,0:T(8,128)(2,1)}), bf16[4,12,2,32,256]{4,3,2,1,0:T(8,128)(2,1)S(1)}, u32[]{:S(2)}, u32[]{:S(2)}) async-start(bf16[4,12,2,32,256]{4,3,2,1,0:T(8,128)(2,1)} %pad_maximum_fusion), calls=%async_computation | async-start | bytes 3145728 | tf_op jit(solution)/shard_map/all_to_all | solution.py:15
  31.0 6.8 %copy-start.6 = (s32[4]{0:T(128)S(1)}, s32[4]{0:T(128)}, u32[]{:S(2)}) copy-start(s32[4]{0:T(128)} %param.15) | copy-start | bytes 52
  32.1 17.4 %collective-permute-start = (bf16[4,2,128,256]{3,2,1,0:T(8,128)(2,1)}, bf16[4,2,128,256]{3,2,1,0:T(8,128)(2,1)S(1)}, u32[]{:S(2)}, u32[]{:S(2)}) collective-permute-start(bf16[4,2,128,256]{3,2,1,0:T(8,128)(2,1)} %get-tuple-element.141), channel_id=1, source_target_pairs={{0,4},{4,8},{8,12},{12,0},{1,5},{5,9},{9,13},{13,1},{2,6},{6,10},{... | collective-permute-start | bytes 1572872 | tf_op jit(solution)/shard_map/ppermute | solution.py:22
  34.4 24.7 %collective-permute-start.2 = (bf16[4,2,128,256]{3,2,1,0:T(8,128)(2,1)}, bf16[4,2,128,256]{3,2,1,0:T(8,128)(2,1)}, u32[]{:S(2)}, u32[]{:S(2)}) collective-permute-start(bf16[4,2,128,256]{3,2,1,0:T(8,128)(2,1)} %get-tuple-element.142), channel_id=1, source_target_pairs={{0,12},{4,0},{8,4},{12,8},{1,13},{5,1},{9,5},{13,9},{2,14},{6,2},{... | collective-permute-start | bytes 1572872 | tf_op jit(solution)/shard_map/ppermute | solution.py:22
  36.5 45.7 %collective-permute-start.1 = (bf16[4,2,128,256]{3,2,1,0:T(8,128)(2,1)S(1)}, bf16[4,2,128,256]{3,2,1,0:T(8,128)(2,1)}, u32[]{:S(2)}, u32[]{:S(2)}) collective-permute-start(bf16[4,2,128,256]{3,2,1,0:T(8,128)(2,1)S(1)} %get-tuple-element.143), channel_id=1, source_target_pairs={{0,8},{4,12},{8,0},{12,4},{1,9},{5,13},{9,1},{13,5},{2,10},{6,14},... | collective-permute-start | bytes 1572872 | tf_op jit(solution)/shard_map/ppermute | solution.py:22
  49.5 32.7 %copy-start.3 = (bf16[4,2,128,256]{3,2,1,0:T(8,128)(2,1)}, bf16[4,2,128,256]{3,2,1,0:T(8,128)(2,1)S(1)}, u32[]{:S(2)}) copy-start(bf16[4,2,128,256]{3,2,1,0:T(8,128)(2,1)S(1)} %collective-permute-done) | copy-start | bytes 1572868
  84.5 1.2 %copy-start.1 = (f32[2,8,128,128]{3,2,1,0:T(8,128)S(1)}, f32[2,8,128,128]{3,2,1,0:T(8,128)}, u32[]{:S(2)}) copy-start(f32[2,8,128,128]{3,2,1,0:T(8,128)} %convolution_add_fusion) | copy-start | bytes 3145732
